TPU v7x, 512 devices: a whole 4x4x16 slice. The times are simulated.
512 devices in a mesh: pipe: 16 (over z_hi, x, core), tensor: 32 (over z_lo, y).
Axes of the slice: x: 4, y: 4, z: 16 (z_hi: 2, z_lo: 8; z = z_hi * 8 + z_lo), core: 2. Of those that a mesh axis runs over, the one named last changes fastest.
Arguments:
- tokens: bfloat16 [512, 8192], P(None, 'pipe'), may hold values from -6 to 6
- out_grad: bfloat16 [512, 8192], P(None, 'pipe'), may hold values from -6 to 6
- w_gate: bfloat16 [8192, 16384], P('pipe', 'tensor'), may hold values from -0.0625 to 0.0625
- w_up: bfloat16 [8192, 16384], P('pipe', 'tensor'), may hold values from -0.0625 to 0.0625
- w_down: bfloat16 [16384, 8192], P('tensor', 'pipe'), may hold values from -0.046875 to 0.046875
Outputs:
- input_grad: float32 [512, 8192], P('tensor', 'pipe')
- gate_mantissa: bfloat16 [8192, 16384], P('pipe', 'tensor')
- gate_scales: float32 [256, 8192], P('pipe', 'tensor')
- up_mantissa: bfloat16 [8192, 16384], P('pipe', 'tensor')
- up_scales: float32 [256, 8192], P('pipe', 'tensor')
- down_mantissa: bfloat16 [16384, 8192], P('tensor', 'pipe')
- down_scales: float32 [8192, 256], P('tensor', 'pipe')
All inputs are finite; a program needn't handle non-finite values.
Results may differ from a plain program's by a relative error of at most 0.0049.
Values may be sent and summed in bfloat16 or wider, within the bound.
No kernel may reach another device: no remote copies, remote signals or barrier semaphores. Data moves between devices by JAX's collectives and lax.ppermute only.
A program may use at most 64 MiB of HBM per device.

v0:
```python
import jax
import jax.numpy as jnp
import numpy as np
from jax import lax
from jax.sharding import Mesh
from jax.sharding import PartitionSpec as P

PIPE_MODE = "hier"
TENSOR_MODE = "zlo_y"
PIPE = ("z_hi", "x", "core")
TENSOR = ("z_lo", "y")


def quantize_features(grad):
    rows, cols = grad.shape
    blocks = grad.reshape(rows // 32, 32, cols // 2, 2)
    scales = jnp.max(jnp.abs(blocks), axis=(1, 3)) + 1e-06
    mantissa = (blocks / scales[:, None, :, None]).reshape(grad.shape)
    return (mantissa.astype(jnp.bfloat16), scales)


def quantize_hidden(grad):
    rows, cols = grad.shape
    blocks = grad.reshape(rows // 2, 2, cols // 32, 32)
    scales = jnp.max(jnp.abs(blocks), axis=(1, 3)) + 1e-06
    mantissa = (blocks / scales[:, None, :, None]).reshape(grad.shape)
    return (mantissa.astype(jnp.bfloat16), scales)


def contract_last(left, right):
    return lax.dot_general(
        left, right, (((1,), (1,)), ((), ())), preferred_element_type=jnp.float32
    )


def contract_first(left, right):
    return lax.dot_general(
        left, right, (((0,), (0,)), ((), ())), preferred_element_type=jnp.float32
    )


def gate_terms(gate, up, hidden_grad):
    sigmoid_gate = jax.nn.sigmoid(gate)
    silu_gate = gate * sigmoid_gate
    hidden = (silu_gate * up).astype(jnp.bfloat16)
    gate_grad = (hidden_grad * up * sigmoid_gate * (1.0 + gate * (1.0 - sigmoid_gate))).astype(
        jnp.bfloat16
    )
    up_grad = (hidden_grad * silu_gate).astype(jnp.bfloat16)
    return (hidden, gate_grad, up_grad)


def pipe_exchange(parts):
    if PIPE_MODE == "flat_ar":
        gate, up, hidden_grad = lax.psum(tuple(parts), PIPE)
        return gate_terms(gate, up, hidden_grad)
    stacked = jnp.stack(parts)
    if PIPE_MODE == "flat":
        shard = lax.psum_scatter(stacked, PIPE, scatter_dimension=1, tiled=True)
    else:
        shard = stacked
        for axis in ("core", "x", "z_hi"):
            shard = lax.psum_scatter(shard, axis, scatter_dimension=1, tiled=True)
    products = jnp.stack(gate_terms(shard[0], shard[1], shard[2]))
    if PIPE_MODE == "flat":
        full = lax.all_gather(products, PIPE, axis=1, tiled=True)
    else:
        full = products
        for axis in ("z_hi", "x", "core"):
            full = lax.all_gather(full, axis, axis=1, tiled=True)
    return (full[0], full[1], full[2])


def tensor_exchange(partial, n_zlo, n_y):
    if TENSOR_MODE == "flat":
        return lax.psum_scatter(partial, TENSOR, scatter_dimension=0, tiled=True)
    if TENSOR_MODE == "zlo_y":
        partial = lax.psum_scatter(partial, "z_lo", scatter_dimension=0, tiled=True)
        return lax.psum_scatter(partial, "y", scatter_dimension=0, tiled=True)
    rows, cols = partial.shape
    blocks = partial.reshape(n_zlo, n_y, rows // (n_zlo * n_y), cols)
    blocks = jnp.swapaxes(blocks, 0, 1).reshape(rows, cols)
    blocks = lax.psum_scatter(blocks, "y", scatter_dimension=0, tiled=True)
    return lax.psum_scatter(blocks, "z_lo", scatter_dimension=0, tiled=True)


def make_on_device(n_zlo, n_y):

    def on_device(tokens, out_grad, w_gate, w_up, w_down):
        gate_part = jnp.dot(tokens, w_gate, preferred_element_type=jnp.float32)
        up_part = jnp.dot(tokens, w_up, preferred_element_type=jnp.float32)
        hidden_part = contract_last(out_grad, w_down)
        hidden, gate_grad, up_grad = pipe_exchange((gate_part, up_part, hidden_part))
        input_grad = tensor_exchange(
            contract_last(gate_grad, w_gate) + contract_last(up_grad, w_up), n_zlo, n_y
        )
        gate_mantissa, gate_scales = quantize_features(contract_first(tokens, gate_grad))
        up_mantissa, up_scales = quantize_features(contract_first(tokens, up_grad))
        down_mantissa, down_scales = quantize_hidden(contract_first(hidden, out_grad))
        return (
            input_grad,
            gate_mantissa,
            gate_scales,
            up_mantissa,
            up_scales,
            down_mantissa,
            down_scales,
        )

    return on_device


def fine_mesh(mesh):
    n_pipe, n_tensor = (mesh.shape["pipe"], mesh.shape["tensor"])
    n_y = 4
    n_zlo = n_tensor // n_y
    n_core = 2
    n_x = 4
    n_zhi = n_pipe // (n_core * n_x)
    devices = np.asarray(mesh.devices).reshape(n_zhi, n_x, n_core, n_zlo, n_y)
    return (Mesh(devices, ("z_hi", "x", "core", "z_lo", "y")), n_zlo, n_y)


def solution(mesh):
    fine, n_zlo, n_y = fine_mesh(mesh)
    in_specs = (P(None, PIPE), P(None, PIPE), P(PIPE, TENSOR), P(PIPE, TENSOR), P(TENSOR, PIPE))
    out_specs = (
        P(TENSOR, PIPE),
        P(PIPE, TENSOR),
        P(PIPE, TENSOR),
        P(PIPE, TENSOR),
        P(PIPE, TENSOR),
        P(TENSOR, PIPE),
        P(TENSOR, PIPE),
    )
    return jax.shard_map(
        make_on_device(n_zlo, n_y),
        mesh=fine,
        in_specs=in_specs,
        out_specs=out_specs,
        check_vma=False,
    )
```

profile of v0, /device:TPU:6, one launch (start us, length us, event | category | flops | bytes accessed | tf_op | source)
XLA Modules:
  0.0 276.1 jit_solution(17815208416039630571)
XLA Ops:
  10.6 1.9 pad_maximum_fusion
  12.6 26.1 %reduce-scatter.6.cloned.1.call-done = f32[3,256,512]{2,1,0:T(8,128)} async-done(((f32[3,512,512]{2,1,0:T(8,128)}), f32[3,256,512]{2,1,0:T(8,128)}) %reduce-scatter.6.cloned.1.call-update) | async-done | bytes 1572880 | tf_op jit(solution)/shard_map/reduce_scatter | solution.py:63
  38.8 36.7 %reduce-scatter.8.cloned.1.call-done = f32[3,64,512]{2,1,0:T(8,128)} async-done(((f32[3,256,512]{2,1,0:T(8,128)}), f32[3,64,512]{2,1,0:T(8,128)}) %reduce-scatter.8.cloned.1.call-update) | async-done | bytes 393232 | tf_op jit(solution)/shard_map/reduce_scatter | solution.py:63
  75.6 48.8 %reduce-scatter.10.cloned.1.call-done = f32[3,32,512]{2,1,0:T(8,128)} async-done(((f32[3,64,512]{2,1,0:T(8,128)}), f32[3,32,512]{2,1,0:T(8,128)}) %reduce-scatter.10.cloned.1.call-update) | async-done | bytes 196624 | tf_op jit(solution)/shard_map/reduce_scatter | solution.py:63
  125.3 17.1 %all_gather.9 = bf16[3,64,512]{2,1,0:T(8,128)(2,1)S(1)} all-gather(bf16[3,32,512]{2,1,0:T(8,128)(2,1)S(1)} %pad_maximum_fusion.1), channel_id=1, replica_groups=mesh['z_hi'=2,'x'=4,'core'=2,'z_lo'=8,'y'=4] {'z_hi'}, dimensions={1}, use_global_device_ids=true | all-gather | bytes 294912 | tf_op jit(solution)/shard_map/all_gather | solution.py:70
  142.4 15.0 %all_gather.10 = bf16[3,256,512]{2,1,0:T(8,128)(2,1)} all-gather(bf16[3,64,512]{2,1,0:T(8,128)(2,1)S(1)} %all_gather.9), channel_id=1, replica_groups=mesh['z_hi'=2,'x'=4,'core'=2,'z_lo'=8,'y'=4] {'x'}, dimensions={1}, use_global_device_ids=true | all-gather | bytes 983040 | tf_op jit(solution)/shard_map/all_gather | solution.py:70
  158.5 12.8 %all-gather.2.cloned.1.call-done = bf16[3,512,512]{2,1,0:T(8,128)(2,1)} async-done(((bf16[3,256,512]{2,1,0:T(8,128)(2,1)}), bf16[3,512,512]{2,1,0:T(8,128)(2,1)}) %all-gather.2.cloned.1.call-update) | async-done | bytes 1572880 | tf_op jit(solution)/shard_map/all_gather | solution.py:70
  171.3 1.6 fusion.2
  176.1 2.5 abs.16
  178.6 2.8 %reduce_max.27 = f32[16,256]{0,1:T(8,128)S(1)} reduce(f32[16,32,256,2]{1,0,3,2:T(8,128)} %abs.16, f32[]{:T(128)} %constant.0.clone.1), dimensions={1,3}, to_apply=%region_5.0 | reduce | flops 258048 | bytes 1064964 | tf_op jit(solution)/shard_map/reduce_max | solution.py:17
  182.1 2.5 div.37
  184.7 4.5 %div.38 = f32[512,512]{0,1:T(8,128)} reshape(f32[16,32,256,2]{1,0,3,2:T(8,128)} %div.37) | data formatting | bytes 2097152 | tf_op jit(solution)/shard_map/div | solution.py:18
  189.1 2.2 divide_convert_fusion.2
  191.4 2.1 copy.30
  194.9 2.5 abs.18
  197.4 2.8 %reduce_max.28 = f32[16,256]{0,1:T(8,128)S(1)} reduce(f32[16,32,256,2]{1,0,3,2:T(8,128)} %abs.18, f32[]{:T(128)} %constant.0.clone.1), dimensions={1,3}, to_apply=%region_6.0 | reduce | flops 258048 | bytes 1064964 | tf_op jit(solution)/shard_map/reduce_max | solution.py:17
  200.9 2.5 div.40
  203.4 4.5 %div.41 = f32[512,512]{0,1:T(8,128)} reshape(f32[16,32,256,2]{1,0,3,2:T(8,128)} %div.40) | data formatting | bytes 2097152 | tf_op jit(solution)/shard_map/div | solution.py:18
  207.9 2.2 divide_convert_fusion.1
  210.1 2.1 copy.32
  213.2 30.7 %reduce-scatter.12.cloned.1.call-done = f32[64,512]{1,0:T(8,128)} async-done(((f32[512,512]{1,0:T(8,128)}), f32[64,512]{1,0:T(8,128)}) %reduce-scatter.12.cloned.1.call-update) | async-done | bytes 131088 | tf_op jit(solution)/shard_map/reduce_scatter | solution.py:78
  244.0 3.0 %copy.29 = bf16[256,2,16,32]{3,2,1,0:T(8,128)(2,1)S(1)} copy(bf16[256,2,16,32]{0,3,2,1:T(8,128)(2,1)S(1)} %divide_convert_fusion) | data formatting | bytes 1048576 | tf_op jit(solution)/shard_map/convert_element_type | solution.py:27
  247.1 2.8 convert_element_type.30
  249.8 19.5 %reduce-scatter.14.cloned.1.call-done = f32[16,512]{1,0:T(8,128)} async-done(((f32[64,512]{1,0:T(8,128)}), f32[16,512]{1,0:T(8,128)}) %reduce-scatter.14.cloned.1.call-update) | async-done | bytes 32784 | tf_op jit(solution)/shard_map/reduce_scatter | solution.py:79
  (51 shorter events, 12.7 us)
Async XLA Ops:
  7.2 1.0 copy-start
  7.2 2.5 copy-start.5
  7.2 2.9 %copy-start.4 = (bf16[512,512]{1,0:T(8,128)(2,1)S(1)}, bf16[512,512]{1,0:T(8,128)(2,1)}, u32[]{:S(2)}) copy-start(bf16[512,512]{1,0:T(8,128)(2,1)} %param.6) | copy-start | bytes 1572868
  7.2 2.9 %copy-start.8 = (bf16[512,512]{1,0:T(8,128)(2,1)S(1)}, bf16[512,512]{1,0:T(8,128)(2,1)}, u32[]{:S(2)}) copy-start(bf16[512,512]{1,0:T(8,128)(2,1)} %param.9) | copy-start | bytes 1572868
  7.2 31.5 %reduce-scatter.6.cloned.1.call-start = ((), (), s32[]{:S(2)}) async-start(), calls=%async_computation.5 | async-start | bytes 4718592 | tf_op jit(solution)/shard_map/reduce_scatter | solution.py:63
  12.6 62.9 %reduce-scatter.8.cloned.1.call-start = ((), (), s32[]{:S(2)}) async-start(), calls=%async_computation.6 | async-start | bytes 1966080 | tf_op jit(solution)/shard_map/reduce_scatter | solution.py:63
  38.8 85.5 %reduce-scatter.10.cloned.1.call-start = ((), (), s32[]{:S(2)}) async-start(), calls=%async_computation.7 | async-start | bytes 589824 | tf_op jit(solution)/shard_map/reduce_scatter | solution.py:63
  75.5 95.8 %all-gather.2.cloned.1.call-start = ((), (), s32[]{:S(2)}) async-start(), calls=%async_computation.8 | async-start | bytes 2359296 | tf_op jit(solution)/shard_map/all_gather | solution.py:70
  157.4 15.5 %copy-start.6 = (bf16[512,512]{1,0:T(8,128)(2,1)S(1)}, bf16[512,512]{1,0:T(8,128)(2,1)}, u32[]{:S(2)}) copy-start(bf16[512,512]{1,0:T(8,128)(2,1)} %param.8) | copy-start | bytes 1572868
  157.4 86.5 %reduce-scatter.12.cloned.1.call-start = ((), (), s32[]{:S(2)}) async-start(), calls=%async_computation.9 | async-start | bytes 1179648 | tf_op jit(solution)/shard_map/reduce_scatter | solution.py:78
  171.3 1.6 copy-start.1
  174.4 94.9 %reduce-scatter.14.cloned.1.call-start = ((), (), s32[]{:S(2)}) async-start(), calls=%async_computation.10 | async-start | bytes 163840 | tf_op jit(solution)/shard_map/reduce_scatter | solution.py:79
  184.7 4.5 %copy-start.3 = (f32[512,512]{0,1:T(8,128)S(1)}, f32[512,512]{0,1:T(8,128)}, u32[]{:S(2)}) copy-start(f32[512,512]{0,1:T(8,128)} %get-tuple-element.32) | copy-start | bytes 3145732
  203.4 4.5 %copy-start.2 = (f32[512,512]{0,1:T(8,128)S(1)}, f32[512,512]{0,1:T(8,128)}, u32[]{:S(2)}) copy-start(f32[512,512]{0,1:T(8,128)} %get-tuple-element.34) | copy-start | bytes 3145732
  210.1 2.6 copy-start.7
  213.2 33.8 %copy-start.9 = (f32[256,16]{0,1:T(8,128)}, f32[256,16]{0,1:T(8,128)S(1)}, u32[]{:S(2)}) copy-start(f32[256,16]{0,1:T(8,128)S(1)} %broadcast_add_fusion.2) | copy-start | bytes 49156
Sparse Core Ops, SparseCore 0:
  12.7 25.9 reduce-scatter.5
  41.6 33.8 reduce-scatter.7
  78.3 45.9 reduce-scatter.9
  157.5 13.7 all-gather.1
  174.5 69.3 reduce-scatter.11
  247.1 22.1 reduce-scatter.13
where the time goes:
time: 277 us; the launch traced here: 276 us
  waiting for transfers between devices  175 us (63%)
  local copies, waits for them, and re-layouts  32.7 us (12%)
  blocking collectives  32.1 us (12%)
  between operations  14.3 us (5%)
  other arithmetic  13.1 us (5%)
  matrix products  8.85 us (3%)
    reduce_scatter x3, waiting for transfers between devices, pipe_exchange(): shard = lax.psum_scatter(shard, axis, scatter_dimension=1, tiled=True)  112 us
    all_gather x2, blocking collectives, pipe_exchange(): full = lax.all_gather(full, axis, axis=1, tiled=True)  32.1 us
    reduce_scatter x1, waiting for transfers between devices, tensor_exchange(): partial = lax.psum_scatter(partial, 'z_lo', scatter_dimension=0, tiled=True)  30.7 us
    reduce_scatter x1, waiting for transfers between devices, tensor_exchange(): return lax.psum_scatter(partial, 'y', scatter_dimension=0, tiled=True)  19.5 us
    div x4, local copies, waits for them, and re-layouts, quantize_features(): mantissa = (blocks / scales[:, None, :, None]).reshape(grad.shape)  14.1 us
    all_gather x1, waiting for transfers between devices, pipe_exchange(): full = lax.all_gather(full, axis, axis=1, tiled=True)  12.8 us
    unnamed x25, local copies, waits for them, and re-layouts  7.51 us
    convert_element_type x2, local copies, waits for them, and re-layouts, quantize_hidden(): return (mantissa.astype(jnp.bfloat16), scales)  5.76 us
  transfers between devices with their start and end apart: 6, of which 6 were waited for; matrix products, arithmetic and copies ran while one was open for 16% of the time, Pallas kernels for 0%

commit v1 on v0

--- a/solution.py
+++ b/solution.py
@@ -67,7 +67,9 @@
     else:
         full = products
         for axis in ("z_hi", "x", "core"):
-            full = lax.all_gather(full, axis, axis=1, tiled=True)
+            full = jnp.concatenate(
+                lax.all_to_all(jnp.stack([full] * lax.axis_size(axis)), axis, 0, 0), axis=1
+            )
     return (full[0], full[1], full[2])
 
 

time: 277 us -> 266 us (0.960)
  blocking collectives: 32.1 us -> 23.1 us
  starting transfers between devices: 0.42 us -> 5.14 us
  waiting for transfers between devices: 175 us -> 171 us
  other arithmetic: 13.1 us -> 10.1 us
    all_gather x2 -> x0, blocking collectives: 32.1 us -> none  [pipe_exchange(): full = lax.all_gather(full, axis, axis=1, tiled=True)]
    all_to_all x0 -> x2, blocking collectives: none -> 23.1 us  [pipe_exchange(): lax.all_to_all(jnp.stack([full] * lax.axis_size(axis)), axis, 0, 0)]
    all_gather x1 -> x0, waiting for transfers between devices: 12.8 us -> none  [pipe_exchange(): full = lax.all_gather(full, axis, axis=1, tiled=True)]
    all_to_all x0 -> x1, waiting for transfers between devices: none -> 6.4 us  [pipe_exchange(): lax.all_to_all(jnp.stack([full] * lax.axis_size(axis)), axis, 0, 0)]
    all_to_all x0 -> x1, starting transfers between devices: none -> 4.8 us  [pipe_exchange(): lax.all_to_all(jnp.stack([full] * lax.axis_size(axis)), axis, 0, 0)]
    reduce_scatter x1, waiting for transfers between devices: 30.7 us -> 34.2 us  [tensor_exchange(): partial = lax.psum_scatter(partial, 'z_lo', scatter_dimension=0, tiled=True)]
    convert_element_type x2, other arithmetic: 4.43 us -> 1.24 us  [quantize_features(): return (mantissa.astype(jnp.bfloat16), scales)]
    unnamed x25 -> x19, local copies, waits for them, and re-layouts: 7.51 us -> 6.42 us
  transfers between devices with their start and end apart: 6 -> 6, of which waited for: 6 -> 6; matrix products, arithmetic and copies ran while one was open for 16% -> 15% of each run, Pallas kernels for 0% -> 0%
where the time goes in v1:
time: 266 us; the launch traced here: 265 us
  waiting for transfers between devices  171 us (64%)
  local copies, waits for them, and re-layouts  32.8 us (12%)
  blocking collectives  23.1 us (9%)
  between operations  14 us (5%)
  other arithmetic  10.1 us (4%)
  matrix products  8.78 us (3%)
  starting transfers between devices  5.14 us (2%)
    reduce_scatter x3, waiting for transfers between devices, pipe_exchange(): shard = lax.psum_scatter(shard, axis, scatter_dimension=1, tiled=True)  112 us
    reduce_scatter x1, waiting for transfers between devices, tensor_exchange(): partial = lax.psum_scatter(partial, 'z_lo', scatter_dimension=0, tiled=True)  34.2 us
    all_to_all x2, blocking collectives, pipe_exchange(): lax.all_to_all(jnp.stack([full] * lax.axis_size(axis)), axis, 0, 0)  23.1 us
    reduce_scatter x1, waiting for transfers between devices, tensor_exchange(): return lax.psum_scatter(partial, 'y', scatter_dimension=0, tiled=True)  19.1 us
    div x4, local copies, waits for them, and re-layouts, quantize_features(): mantissa = (blocks / scales[:, None, :, None]).reshape(grad.shape)  12.3 us
    unnamed x19, local copies, waits for them, and re-layouts  6.42 us
    all_to_all x1, waiting for transfers between devices, pipe_exchange(): lax.all_to_all(jnp.stack([full] * lax.axis_size(axis)), axis, 0, 0)  6.4 us
    convert_element_type x2, local copies, waits for them, and re-layouts, quantize_hidden(): return (mantissa.astype(jnp.bfloat16), scales)  5.76 us
  transfers between devices with their start and end apart: 6, of which 6 were waited for; matrix products, arithmetic and copies ran while one was open for 15% of the time, Pallas kernels for 0%

profile of v1, /device:TPU:6, one launch (start us, length us, event | category | flops | bytes accessed | tf_op | source)
XLA Modules:
  0.0 265.2 jit_solution(17156080661338140297)
XLA Ops:
  8.2 1.5 convolution_bitcast_fusion.3
  9.7 1.5 convolution_bitcast_fusion.4
  11.7 2.0 pad_maximum_fusion
  13.7 26.1 %reduce-scatter.6.cloned.1.call-done = f32[3,256,512]{2,1,0:T(8,128)} async-done(((f32[3,512,512]{2,1,0:T(8,128)}), f32[3,256,512]{2,1,0:T(8,128)}) %reduce-scatter.6.cloned.1.call-update) | async-done | bytes 1572880 | tf_op jit(solution)/shard_map/reduce_scatter | solution.py:63
  39.9 36.7 %reduce-scatter.8.cloned.1.call-done = f32[3,64,512]{2,1,0:T(8,128)} async-done(((f32[3,256,512]{2,1,0:T(8,128)}), f32[3,64,512]{2,1,0:T(8,128)}) %reduce-scatter.8.cloned.1.call-update) | async-done | bytes 393232 | tf_op jit(solution)/shard_map/reduce_scatter | solution.py:63
  76.6 48.8 %reduce-scatter.10.cloned.1.call-done = f32[3,32,512]{2,1,0:T(8,128)} async-done(((f32[3,64,512]{2,1,0:T(8,128)}), f32[3,32,512]{2,1,0:T(8,128)}) %reduce-scatter.10.cloned.1.call-update) | async-done | bytes 196624 | tf_op jit(solution)/shard_map/reduce_scatter | solution.py:63
  126.4 18.0 %all_to_all.15 = bf16[2,3,32,512]{3,2,1,0:T(8,128)(2,1)S(1)} all-to-all(bf16[2,3,32,512]{3,2,1,0:T(8,128)(2,1)S(1)} %pad_maximum_fusion.2), channel_id=1, replica_groups=mesh['z_hi'=2,'x'=4,'core'=2,'z_lo'=8,'y'=4] {'z_hi'}, dimensions={0} | all-to-all | bytes 393216 | tf_op jit(solution)/shard_map/all_to_all | solution.py:71
  145.3 4.8 %all-to-all-start.1 = ((bf16[4,3,64,512]{3,2,1,0:T(8,128)(2,1)}), bf16[4,3,64,512]{3,2,1,0:T(8,128)(2,1)S(1)}, u32[]{:S(2)}, u32[]{:S(2)}) async-start(bf16[4,3,64,512]{3,2,1,0:T(8,128)(2,1)} %stack.38), calls=%async_computation.4 | async-start | bytes 1572864 | tf_op jit(solution)/shard_map/all_to_all | solution.py:71
  151.1 6.4 %all-to-all-done.1 = bf16[4,3,64,512]{3,2,1,0:T(8,128)(2,1)S(1)} async-done(((bf16[4,3,64,512]{3,2,1,0:T(8,128)(2,1)}), bf16[4,3,64,512]{3,2,1,0:T(8,128)(2,1)S(1)}, u32[]{:S(2)}, u32[]{:S(2)}) %all-to-all-start.1) | async-done | bytes 786464 | tf_op jit(solution)/shard_map/all_to_all | solution.py:71
  157.8 5.1 %all_to_all.16 = bf16[2,3,256,512]{3,2,1,0:T(8,128)(2,1)S(1)} all-to-all(bf16[2,3,256,512]{3,2,1,0:T(8,128)(2,1)S(1)} %pad_maximum_fusion.1), channel_id=1, replica_groups=mesh['z_hi'=2,'x'=4,'core'=2,'z_lo'=8,'y'=4] {'core'}, dimensions={0} | all-to-all | bytes 3145728 | tf_op jit(solution)/shard_map/all_to_all | solution.py:71
  167.4 2.5 abs.16
  169.9 2.8 %reduce_max.27 = f32[16,256]{0,1:T(8,128)S(1)} reduce(f32[16,32,256,2]{1,0,3,2:T(8,128)} %abs.16, f32[]{:T(128)} %constant.0.clone.1), dimensions={1,3}, to_apply=%region_5.0 | reduce | flops 258048 | bytes 1064964 | tf_op jit(solution)/shard_map/reduce_max | solution.py:17
  173.4 2.5 div.37
  176.0 3.6 %div.38 = f32[512,512]{0,1:T(8,128)S(1)} reshape(f32[16,32,256,2]{1,0,3,2:T(8,128)} %div.37) | data formatting | bytes 2097152 | tf_op jit(solution)/shard_map/div | solution.py:18
  180.6 2.0 copy.32
  183.1 2.5 abs.18
  185.6 2.8 %reduce_max.28 = f32[16,256]{0,1:T(8,128)S(1)} reduce(f32[16,32,256,2]{1,0,3,2:T(8,128)} %abs.18, f32[]{:T(128)} %constant.0.clone.1), dimensions={1,3}, to_apply=%region_6.0 | reduce | flops 258048 | bytes 1064964 | tf_op jit(solution)/shard_map/reduce_max | solution.py:17
  189.2 2.5 div.40
  191.7 3.5 %div.41 = f32[512,512]{0,1:T(8,128)S(1)} reshape(f32[16,32,256,2]{1,0,3,2:T(8,128)} %div.40) | data formatting | bytes 2097152 | tf_op jit(solution)/shard_map/div | solution.py:18
  198.0 1.5 abs_reduce_fusion
  199.5 34.2 %reduce-scatter.12.cloned.1.call-done = f32[64,512]{1,0:T(8,128)} async-done(((f32[512,512]{1,0:T(8,128)}), f32[64,512]{1,0:T(8,128)}) %reduce-scatter.12.cloned.1.call-update) | async-done | bytes 131088 | tf_op jit(solution)/shard_map/reduce_scatter | solution.py:80
  233.9 3.0 %copy.31 = bf16[256,2,16,32]{3,2,1,0:T(8,128)(2,1)S(1)} copy(bf16[256,2,16,32]{0,3,2,1:T(8,128)(2,1)S(1)} %divide_convert_fusion) | data formatting | bytes 1048576 | tf_op jit(solution)/shard_map/convert_element_type | solution.py:27
  236.9 2.8 %convert_element_type.30 = bf16[512,512]{1,0:T(8,128)(2,1)} reshape(bf16[256,2,16,32]{3,2,1,0:T(8,128)(2,1)S(1)} %copy.31) | data formatting | bytes 1048576 | tf_op jit(solution)/shard_map/convert_element_type | solution.py:27
  239.6 19.1 %reduce-scatter.14.cloned.1.call-done = f32[16,512]{1,0:T(8,128)} async-done(((f32[64,512]{1,0:T(8,128)}), f32[16,512]{1,0:T(8,128)}) %reduce-scatter.14.cloned.1.call-update) | async-done | bytes 32784 | tf_op jit(solution)/shard_map/reduce_scatter | solution.py:81
  (49 shorter events, 15.0 us)
Async XLA Ops:
  7.2 1.0 copy-start
  7.2 4.0 %copy-start.2 = (bf16[512,512]{1,0:T(8,128)(2,1)S(1)}, bf16[512,512]{1,0:T(8,128)(2,1)}, u32[]{:S(2)}) copy-start(bf16[512,512]{1,0:T(8,128)(2,1)} %param.6) | copy-start | bytes 1572868
  7.2 4.0 %copy-start.5 = (bf16[512,512]{1,0:T(8,128)(2,1)S(1)}, bf16[512,512]{1,0:T(8,128)(2,1)}, u32[]{:S(2)}) copy-start(bf16[512,512]{1,0:T(8,128)(2,1)} %param.9) | copy-start | bytes 1572868
  7.2 32.6 %reduce-scatter.6.cloned.1.call-start = ((), (), s32[]{:S(2)}) async-start(), calls=%async_computation.8 | async-start | bytes 4718592 | tf_op jit(solution)/shard_map/reduce_scatter | solution.py:63
  13.6 62.9 %reduce-scatter.8.cloned.1.call-start = ((), (), s32[]{:S(2)}) async-start(), calls=%async_computation.9 | async-start | bytes 1966080 | tf_op jit(solution)/shard_map/reduce_scatter | solution.py:63
  39.8 85.5 %reduce-scatter.10.cloned.1.call-start = ((), (), s32[]{:S(2)}) async-start(), calls=%async_computation.10 | async-start | bytes 589824 | tf_op jit(solution)/shard_map/reduce_scatter | solution.py:63
  145.3 12.2 %all-to-all-start.1 = ((bf16[4,3,64,512]{3,2,1,0:T(8,128)(2,1)}), bf16[4,3,64,512]{3,2,1,0:T(8,128)(2,1)S(1)}, u32[]{:S(2)}, u32[]{:S(2)}) async-start(bf16[4,3,64,512]{3,2,1,0:T(8,128)(2,1)} %stack.38), calls=%async_computation.4 | async-start | bytes 1572864 | tf_op jit(solution)/shard_map/all_to_all | solution.py:71
  150.1 83.6 %reduce-scatter.12.cloned.1.call-start = ((), (), s32[]{:S(2)}) async-start(), calls=%async_computation.11 | async-start | bytes 1179648 | tf_op jit(solution)/shard_map/reduce_scatter | solution.py:80
  157.8 6.0 %copy-start.3 = (bf16[512,512]{1,0:T(8,128)(2,1)S(1)}, bf16[512,512]{1,0:T(8,128)(2,1)}, u32[]{:S(2)}) copy-start(bf16[512,512]{1,0:T(8,128)(2,1)} %param.7) | copy-start | bytes 1572868
  162.9 1.4 copy-start.4
  165.7 93.0 %reduce-scatter.14.cloned.1.call-start = ((), (), s32[]{:S(2)}) async-start(), calls=%async_computation.12 | async-start | bytes 163840 | tf_op jit(solution)/shard_map/reduce_scatter | solution.py:81
  176.0 3.6 %copy-start.1 = (f32[512,512]{0,1:T(8,128)S(1)}, f32[512,512]{0,1:T(8,128)}, u32[]{:S(2)}) copy-start(f32[512,512]{0,1:T(8,128)} %get-tuple-element.35) | copy-start | bytes 3145732
  199.5 40.1 %copy-start.6 = (f32[256,16]{0,1:T(8,128)}, f32[256,16]{0,1:T(8,128)S(1)}, u32[]{:S(2)}) copy-start(f32[256,16]{0,1:T(8,128)S(1)} %broadcast_add_fusion.2) | copy-start | bytes 49156
Sparse Core Ops, SparseCore 0:
  13.8 25.9 reduce-scatter.5
  42.6 33.8 reduce-scatter.7
  79.3 45.9 reduce-scatter.9
  165.9 67.8 reduce-scatter.11
  236.9 21.7 reduce-scatter.13
